TPU v7x, 256 devices: a whole 4x4x8 slice. The times are simulated.
256 devices in a mesh: hst: 64 (over x, y, z_lo), chip: 4 (over z_hi, core).
Axes of the slice: x: 4, y: 4, z: 8 (z_hi: 2, z_lo: 4; z = z_hi * 4 + z_lo), core: 2. Of those that a mesh axis runs over, the one named last changes fastest.
Arguments:
- points: bfloat16 [131072, 1024], P(('hst', 'chip')), may hold values from -640 to 640
- assign: int32 [131072], P(('hst', 'chip')), may hold values from 0 to 8191, as said below
Outputs:
- centroids: bfloat16 [8192, 1024], P('hst', 'chip')
- nearest: float32 [131072], P(('hst', 'chip'))
Inputs may be any that keep to these rules, and one draw needn't show every extreme that they name: `assign`: cluster o * 128 + j lies in owner block o. Among the 512 points of one device at most 16 name clusters of any one owner block; in every draw one owner block gets exactly 16 points from every device.
All inputs are finite; a program needn't handle non-finite values.
Results may differ from a plain program's by a relative error of at most 0.0095.
Values may be sent and summed in bfloat16 or wider, within the bound.
No kernel may reach another device: no remote copies, remote signals or barrier semaphores. Data moves between devices by JAX's collectives and lax.ppermute only.
A program may use at most 64 MiB of HBM per device.

v0:
```python
import jax
import jax.numpy as jnp
from jax import lax
from jax.sharding import PartitionSpec as P

K_HOST = 128
CYCLE = 8
EPSILON = 1e-06


def shifted(block, axis, distance):
    devices = range(lax.axis_size(axis))
    route = [((i - distance) % len(devices), i) for i in devices]
    return lax.ppermute(block, axis, route)


def cluster_sums(values, labels, row_count):
    stride = min(row_count, 1024)

    def one_block(offset):
        wanted = offset + jnp.arange(stride, dtype=jnp.int32)
        member = (wanted[:, None] == labels[None, :]).astype(jnp.bfloat16)
        return jnp.dot(member, values, preferred_element_type=jnp.float32)

    offsets = jnp.arange(row_count // stride, dtype=jnp.int32) * stride
    return lax.map(one_block, offsets).reshape(row_count, values.shape[1])


def body(points, assign):
    feature_count = points.shape[1]
    chip_count = lax.axis_size("chip")
    chip_index = lax.axis_index("chip")
    quarter = feature_count // chip_count
    host_points, host_labels = (
        lax.all_gather(points, "chip", axis=0, tiled=True),
        lax.all_gather(assign, "chip", axis=0, tiled=True),
    )
    columns = lax.dynamic_slice_in_dim(host_points, chip_index * quarter, quarter, 1)
    shares = lax.psum_scatter(
        cluster_sums(columns, host_labels, K_HOST * lax.axis_size("hst")),
        "hst",
        scatter_dimension=0,
        tiled=True,
    )
    squares = lax.psum(jnp.sum(shares * shares, axis=1), "chip")
    factor = lax.rsqrt(squares / feature_count + EPSILON)
    centroids = (shares * factor[:, None]).astype(jnp.bfloat16)
    own_block = lax.all_gather(centroids, "chip", axis=1, tiled=True)
    widened = points.astype(jnp.float32)
    unit_points = (
        widened * lax.rsqrt(jnp.mean(widened * widened, axis=1, keepdims=True) + EPSILON)
    ).astype(jnp.bfloat16)

    def nearest_in(candidates):
        scores = jnp.einsum(
            "pd,kd->pk", unit_points, candidates, preferred_element_type=jnp.float32
        )
        return jnp.min(2.0 - 2.0 * scores / feature_count, axis=1)

    nearest = nearest_in(own_block)
    moving = own_block
    for section_index in range(CYCLE - 1):
        moving = shifted(moving, "hst", 1)
        nearest = jnp.minimum(nearest, nearest_in(moving))
    return (centroids, nearest)


def solution(mesh):
    in_specs = (P(("hst", "chip"), None), P(("hst", "chip")))
    out_specs = (P("hst", "chip"), P(("hst", "chip")))
    return jax.shard_map(body, mesh=mesh, in_specs=in_specs, out_specs=out_specs, check_vma=False)
```

profile of v0, /device:TPU:0, one launch (start us, length us, event | category | flops | bytes accessed | tf_op | source)
XLA Modules:
  0.0 626.2 jit_solution(5738999434727934108)
XLA Ops:
  8.0 9.2 %all-gather = s32[4,1,512]{2,1,0:T(1,128)S(1)} all-gather(s32[1,1,512]{2,1,0:T(1,128)} %bitcast.25), channel_id=1, replica_groups=mesh['hst'=64,'chip'=4] {'chip'}, dimensions={0}, use_global_device_ids=true | all-gather | bytes 10240 | tf_op jit(solution)/shard_map/all_gather | solution.py:36
  17.2 60.4 %all-gather.3.cloned.1.call-done = bf16[2048,1024]{1,0:T(8,128)(2,1)} async-done(((bf16[512,1024]{1,0:T(8,128)(2,1)}), bf16[2048,1024]{1,0:T(8,128)(2,1)}) %all-gather.3.cloned.1.call-update) | async-done | bytes 4194320 | tf_op jit(solution)/shard_map/all_gather | solution.py:35
  77.6 1.3 constant_dynamic-slice_fusion
  78.9 28.5 %while.10 = (s32[]{:T(128)}, f32[8,1024,256]{2,1,0:T(8,128)}, s32[8]{0:T(128)S(1)}, s32[2048]{0:T(1024)S(1)}, bf16[2048,256]{1,0:T(8,128)(2,1)S(1)}, /*index=5*/s32[]{:T(128)}) while((s32[]{:T(128)}, f32[8,1024,256]{2,1,0:T(8,128)}, s32[8]{0:T(128)S(1)}, s32[2048]{0:T(1024)S(1)}, bf16[2048,256]{1,0:T(8,128)(2,1)S(1)}, ...), condition=%wide.region_1.2_spmd, body=%wide.region_0.1_spmd.sunk | while | flops 1075840000 | bytes 2114133 | solution.py:26
  80.1 2.3 fusion.50
  83.7 2.4 fusion.50
  87.3 2.3 fusion.50
  90.8 2.3 fusion.50
  94.4 2.3 fusion.50
  97.9 2.3 fusion.50
  101.5 2.3 fusion.50
  105.1 2.3 fusion.50
  107.4 398.8 %reduce-scatter.2.cloned.1.call-done = f32[128,256]{1,0:T(8,128)} async-done(((f32[8192,256]{1,0:T(8,128)}), f32[128,256]{1,0:T(8,128)}) %reduce-scatter.2.cloned.1.call-update) | async-done | bytes 131088 | tf_op jit(solution)/shard_map/reduce_scatter | solution.py:39
  506.2 1.0 multiply_reduce_fusion
  507.2 9.6 %psum.7 = f32[128]{0:T(128)S(1)} all-reduce(f32[128]{0:T(128)S(1)} %multiply_reduce_fusion), channel_id=1, replica_groups=mesh['hst'=64,'chip'=4] {'chip'}, use_global_device_ids=true, to_apply=%region_4.5 | all-reduce | flops 128 | bytes 1024 | tf_op jit(solution)/shard_map/psum | solution.py:45
  516.8 1.0 multiply_convert_fusion
  517.8 9.7 %all_gather.11 = bf16[128,1024]{1,0:T(8,128)(2,1)S(1)} all-gather(bf16[128,256]{1,0:T(8,128)(2,1)S(1)} %multiply_convert_fusion), channel_id=1, replica_groups=mesh['hst'=64,'chip'=4] {'chip'}, dimensions={1}, use_global_device_ids=true | all-gather | bytes 327680 | tf_op jit(solution)/shard_map/all_gather | solution.py:48
  527.5 14.6 %collective-permute-done = bf16[128,1024]{1,0:T(8,128)(2,1)S(1)} collective-permute-done((bf16[128,1024]{1,0:T(8,128)(2,1)S(1)}, bf16[128,1024]{1,0:T(8,128)(2,1)S(1)}, u32[]{:S(2)}, u32[]{:S(2)}) %collective-permute-start) | collective-permute-done | bytes 262176 | tf_op jit(solution)/shard_map/ppermute | solution.py:14
  542.0 13.7 %collective-permute-done.1 = bf16[128,1024]{1,0:T(8,128)(2,1)S(1)} collective-permute-done((bf16[128,1024]{1,0:T(8,128)(2,1)S(1)}, bf16[128,1024]{1,0:T(8,128)(2,1)S(1)}, u32[]{:S(2)}, u32[]{:S(2)}) %collective-permute-start.1) | collective-permute-done | bytes 262176 | tf_op jit(solution)/shard_map/ppermute | solution.py:14
  556.0 12.6 %collective-permute-done.2 = bf16[128,1024]{1,0:T(8,128)(2,1)S(1)} collective-permute-done((bf16[128,1024]{1,0:T(8,128)(2,1)S(1)}, bf16[128,1024]{1,0:T(8,128)(2,1)S(1)}, u32[]{:S(2)}, u32[]{:S(2)}) %collective-permute-start.2) | collective-permute-done | bytes 262176 | tf_op jit(solution)/shard_map/ppermute | solution.py:14
  569.2 11.8 %collective-permute-done.3 = bf16[128,1024]{1,0:T(8,128)(2,1)S(1)} collective-permute-done((bf16[128,1024]{1,0:T(8,128)(2,1)S(1)}, bf16[128,1024]{1,0:T(8,128)(2,1)S(1)}, u32[]{:S(2)}, u32[]{:S(2)}) %collective-permute-start.3) | collective-permute-done | bytes 262176 | tf_op jit(solution)/shard_map/ppermute | solution.py:14
  582.2 11.2 %collective-permute-done.4 = bf16[128,1024]{1,0:T(8,128)(2,1)S(1)} collective-permute-done((bf16[128,1024]{1,0:T(8,128)(2,1)S(1)}, bf16[128,1024]{1,0:T(8,128)(2,1)S(1)}, u32[]{:S(2)}, u32[]{:S(2)}) %collective-permute-start.4) | collective-permute-done | bytes 262176 | tf_op jit(solution)/shard_map/ppermute | solution.py:14
  594.5 11.2 %collective-permute-done.5 = bf16[128,1024]{1,0:T(8,128)(2,1)S(1)} collective-permute-done((bf16[128,1024]{1,0:T(8,128)(2,1)S(1)}, bf16[128,1024]{1,0:T(8,128)(2,1)S(1)}, u32[]{:S(2)}, u32[]{:S(2)}) %collective-permute-start.5) | collective-permute-done | bytes 262176 | tf_op jit(solution)/shard_map/ppermute | solution.py:14
  606.9 11.2 %collective-permute-done.6 = bf16[128,1024]{1,0:T(8,128)(2,1)S(1)} collective-permute-done((bf16[128,1024]{1,0:T(8,128)(2,1)S(1)}, bf16[128,1024]{1,0:T(8,128)(2,1)S(1)}, u32[]{:S(2)}, u32[]{:S(2)}) %collective-permute-start.6) | collective-permute-done | bytes 262176 | tf_op jit(solution)/shard_map/ppermute | solution.py:14
  (45 shorter events, 16.1 us)
Async XLA Ops:
  7.2 70.4 %all-gather.3.cloned.1.call-start = ((), (), s32[]{:S(2)}) async-start(), calls=%async_computation.1 | async-start | bytes 5242880 | tf_op jit(solution)/shard_map/all_gather | solution.py:35
  7.9 498.3 %reduce-scatter.2.cloned.1.call-start = ((), (), s32[]{:S(2)}) async-start(), calls=%async_computation.2 | async-start | bytes 8519680 | tf_op jit(solution)/shard_map/reduce_scatter | solution.py:39
  107.4 448.4 %copy-start = (bf16[512,1024]{1,0:T(8,128)(2,1)S(1)}, bf16[512,1024]{1,0:T(8,128)(2,1)}, u32[]{:S(2)}) copy-start(bf16[512,1024]{1,0:T(8,128)(2,1)} %param.4) | copy-start | bytes 3145732
  517.8 63.8 %copy-start.1 = (bf16[128,256]{1,0:T(8,128)(2,1)}, bf16[128,256]{1,0:T(8,128)(2,1)S(1)}, u32[]{:S(2)}) copy-start(bf16[128,256]{1,0:T(8,128)(2,1)S(1)} %multiply_convert_fusion) | copy-start | bytes 196612
  527.5 14.6 %collective-permute-start = (bf16[128,1024]{1,0:T(8,128)(2,1)S(1)}, bf16[128,1024]{1,0:T(8,128)(2,1)S(1)}, u32[]{:S(2)}, u32[]{:S(2)}) collective-permute-start(bf16[128,1024]{1,0:T(8,128)(2,1)S(1)} %all_gather.11), channel_id=1, source_target_pairs={{252,0},{0,4},{4,8},{8,12},{12,16},{16,20},{20,24},{24,28},{28,32}... | collective-permute-start | bytes 786440 | tf_op jit(solution)/shard_map/ppermute | solution.py:14
  542.0 13.7 %collective-permute-start.1 = (bf16[128,1024]{1,0:T(8,128)(2,1)S(1)}, bf16[128,1024]{1,0:T(8,128)(2,1)S(1)}, u32[]{:S(2)}, u32[]{:S(2)}) collective-permute-start(bf16[128,1024]{1,0:T(8,128)(2,1)S(1)} %collective-permute-done), channel_id=1, source_target_pairs={{252,0},{0,4},{4,8},{8,12},{12,16},{16,20},{20,24},{24,28},{28,32}... | collective-permute-start | bytes 786440 | tf_op jit(solution)/shard_map/ppermute | solution.py:14
  555.7 12.9 %collective-permute-start.2 = (bf16[128,1024]{1,0:T(8,128)(2,1)S(1)}, bf16[128,1024]{1,0:T(8,128)(2,1)S(1)}, u32[]{:S(2)}, u32[]{:S(2)}) collective-permute-start(bf16[128,1024]{1,0:T(8,128)(2,1)S(1)} %collective-permute-done.1), channel_id=1, source_target_pairs={{252,0},{0,4},{4,8},{8,12},{12,16},{16,20},{20,24},{24,28},{28,32}... | collective-permute-start | bytes 786440 | tf_op jit(solution)/shard_map/ppermute | solution.py:14
  568.6 12.4 %collective-permute-start.3 = (bf16[128,1024]{1,0:T(8,128)(2,1)S(1)}, bf16[128,1024]{1,0:T(8,128)(2,1)S(1)}, u32[]{:S(2)}, u32[]{:S(2)}) collective-permute-start(bf16[128,1024]{1,0:T(8,128)(2,1)S(1)} %collective-permute-done.2), channel_id=1, source_target_pairs={{252,0},{0,4},{4,8},{8,12},{12,16},{16,20},{20,24},{24,28},{28,32}... | collective-permute-start | bytes 786440 | tf_op jit(solution)/shard_map/ppermute | solution.py:14
  581.0 12.4 %collective-permute-start.4 = (bf16[128,1024]{1,0:T(8,128)(2,1)S(1)}, bf16[128,1024]{1,0:T(8,128)(2,1)S(1)}, u32[]{:S(2)}, u32[]{:S(2)}) collective-permute-start(bf16[128,1024]{1,0:T(8,128)(2,1)S(1)} %collective-permute-done.3), channel_id=1, source_target_pairs={{252,0},{0,4},{4,8},{8,12},{12,16},{16,20},{20,24},{24,28},{28,32}... | collective-permute-start | bytes 786440 | tf_op jit(solution)/shard_map/ppermute | solution.py:14
  593.4 12.4 %collective-permute-start.5 = (bf16[128,1024]{1,0:T(8,128)(2,1)S(1)}, bf16[128,1024]{1,0:T(8,128)(2,1)S(1)}, u32[]{:S(2)}, u32[]{:S(2)}) collective-permute-start(bf16[128,1024]{1,0:T(8,128)(2,1)S(1)} %collective-permute-done.4), channel_id=1, source_target_pairs={{252,0},{0,4},{4,8},{8,12},{12,16},{16,20},{20,24},{24,28},{28,32}... | collective-permute-start | bytes 786440 | tf_op jit(solution)/shard_map/ppermute | solution.py:14
  605.8 12.4 %collective-permute-start.6 = (bf16[128,1024]{1,0:T(8,128)(2,1)S(1)}, bf16[128,1024]{1,0:T(8,128)(2,1)S(1)}, u32[]{:S(2)}, u32[]{:S(2)}) collective-permute-start(bf16[128,1024]{1,0:T(8,128)(2,1)S(1)} %collective-permute-done.5), channel_id=1, source_target_pairs={{252,0},{0,4},{4,8},{8,12},{12,16},{16,20},{20,24},{24,28},{28,32}... | collective-permute-start | bytes 786440 | tf_op jit(solution)/shard_map/ppermute | solution.py:14
Sparse Core Ops, SparseCore 0:
  9.8 67.7 all-gather.2
  107.5 398.6 reduce-scatter.1
where the time goes:
time: 626 us
  waiting for transfers between devices  546 us (87%)
  blocking collectives  28.5 us (5%)
  matrix products  23.1 us (4%)
  between operations  14.1 us (2%)
  other arithmetic  8.06 us (1%)
    reduce_scatter x1, waiting for transfers between devices, body(): lax.psum_scatter(cluster_sums(columns, host_labels, K_HOST * lax.axis_siz...  399 us
    ppermute x7, waiting for transfers between devices, shifted(): return lax.ppermute(block, axis, route)  86.4 us
    all_gather x1, waiting for transfers between devices, body(): lax.all_gather(points, 'chip', axis=0, tiled=True)  60.4 us
    dot_general x8, matrix products, one_block(): return jnp.dot(member, values, preferred_element_type=jnp.float32)  18.6 us
  transfers between devices with their start and end apart: 9, of which 9 were waited for; matrix products, arithmetic and copies ran while one was open for 1% of the time, Pallas kernels for 0%

commit v1 on v0

--- a/solution.py
+++ b/solution.py
@@ -1,3 +1,4 @@
+import functools
 import jax
 import jax.numpy as jnp
 from jax import lax
@@ -6,6 +7,16 @@
 K_HOST = 128
 CYCLE = 8
 EPSILON = 1e-06
+
+
+def circles_return_all(mat, which_dim):
+    e_now = jnp.stack([mat for _ in range(lax.axis_size("chip"))])
+    answer = lax.all_to_all(e_now, axis_name="chip", split_axis=0, concat_axis=0)
+    mixed_arr = jnp.concatenate(answer, which_dim)
+    return mixed_arr
+
+
+measure_the_row = functools.partial(circles_return_all, which_dim=0)
 
 
 def shifted(block, axis, distance):
@@ -32,7 +43,7 @@
     chip_index = lax.axis_index("chip")
     quarter = feature_count // chip_count
     host_points, host_labels = (
-        lax.all_gather(points, "chip", axis=0, tiled=True),
+        measure_the_row(points),
         lax.all_gather(assign, "chip", axis=0, tiled=True),
     )
     columns = lax.dynamic_slice_in_dim(host_points, chip_index * quarter, quarter, 1)

time: 626 us -> 668 us (1.067)
  blocking collectives: 28.5 us -> 117 us
  waiting for transfers between devices: 546 us -> 489 us
  starting transfers between devices: 0.09 us -> 6.9 us
    all_gather x1, blocking collectives: 9.23 us -> 97.6 us  [body(): lax.all_gather(assign, 'chip', axis=0, tiled=True)]
    all_gather x1 -> x0, waiting for transfers between devices: 60.4 us -> none  [body(): lax.all_gather(points, 'chip', axis=0, tiled=True)]
    all_to_all x0 -> x1, starting transfers between devices: none -> 6.88 us  [circles_return_all(): lax.all_to_all(e_now, axis_name='chip', split_axis=0, concat_axis=0)]
  transfers between devices with their start and end apart: 9 -> 9, of which waited for: 9 -> 8; matrix products, arithmetic and copies ran while one was open for 1% -> 1% of each run, Pallas kernels for 0% -> 0%
where the time goes in v1:
time: 668 us
  waiting for transfers between devices  489 us (73%)
  blocking collectives  117 us (18%)
  matrix products  23.2 us (3%)
  between operations  14.1 us (2%)
  local copies, waits for them, and re-layouts  9.7 us (1%)
  other arithmetic  8.06 us (1%)
  starting transfers between devices  6.9 us (1%)
    reduce_scatter x1, waiting for transfers between devices, body(): lax.psum_scatter(cluster_sums(columns, host_labels, K_HOST * lax.axis_siz...  403 us
    all_gather x1, blocking collectives, body(): lax.all_gather(assign, 'chip', axis=0, tiled=True)  97.6 us
    ppermute x7, waiting for transfers between devices, shifted(): return lax.ppermute(block, axis, route)  86.3 us
    dot_general x8, matrix products, one_block(): return jnp.dot(member, values, preferred_element_type=jnp.float32)  18.6 us
  transfers between devices with their start and end apart: 9, of which 8 were waited for; matrix products, arithmetic and copies ran while one was open for 1% of the time, Pallas kernels for 0%

profile of v1, /device:TPU:0, one launch (start us, length us, event | category | flops | bytes accessed | tf_op | source)
XLA Modules:
  0.0 668.0 jit_solution(3677720346168061699)
XLA Ops:
  7.2 3.7 stack.2
  10.9 6.9 %all-to-all-start = ((bf16[4,512,1024]{2,1,0:T(8,128)(2,1)}), bf16[4,512,1024]{2,1,0:T(8,128)(2,1)}, u32[]{:S(2)}, u32[]{:S(2)}) async-start(bf16[4,512,1024]{2,1,0:T(8,128)(2,1)} %stack.2), calls=%async_computation | async-start | bytes 8388608 | tf_op jit(solution)/shard_map/all_to_all | solution.py:14
  17.8 97.6 %all-gather = s32[4,1,512]{2,1,0:T(1,128)S(1)} all-gather(s32[1,1,512]{2,1,0:T(1,128)S(1)} %bitcast.26), channel_id=1, replica_groups=mesh['hst'=64,'chip'=4] {'chip'}, dimensions={0}, use_global_device_ids=true | all-gather | bytes 10240 | tf_op jit(solution)/shard_map/all_gather | solution.py:47
  115.3 1.3 constant_dynamic-slice_fusion
  116.6 28.5 %while.10 = (s32[]{:T(128)}, f32[8,1024,256]{2,1,0:T(8,128)}, s32[8]{0:T(128)S(1)}, s32[2048]{0:T(1024)S(1)}, bf16[2048,256]{1,0:T(8,128)(2,1)S(1)}, /*index=5*/s32[]{:T(128)}) while((s32[]{:T(128)}, f32[8,1024,256]{2,1,0:T(8,128)}, s32[8]{0:T(128)S(1)}, s32[2048]{0:T(1024)S(1)}, bf16[2048,256]{1,0:T(8,128)(2,1)S(1)}, ...), condition=%wide.region_1.2_spmd, body=%wide.region_0.1_spmd.sunk | while | flops 1075840000 | bytes 2114133 | solution.py:37
  117.9 2.3 fusion.50
  121.4 2.4 fusion.50
  125.0 2.3 fusion.50
  128.6 2.3 fusion.50
  132.1 2.3 fusion.50
  135.7 2.3 fusion.50
  139.3 2.3 fusion.50
  142.8 2.3 fusion.50
  145.1 402.8 %reduce-scatter.2.cloned.1.call-done = f32[128,256]{1,0:T(8,128)} async-done(((f32[8192,256]{1,0:T(8,128)}), f32[128,256]{1,0:T(8,128)}) %reduce-scatter.2.cloned.1.call-update) | async-done | bytes 131088 | tf_op jit(solution)/shard_map/reduce_scatter | solution.py:50
  548.0 1.0 multiply_reduce_fusion
  549.0 9.6 %psum.7 = f32[128]{0:T(128)S(1)} all-reduce(f32[128]{0:T(128)S(1)} %multiply_reduce_fusion), channel_id=1, replica_groups=mesh['hst'=64,'chip'=4] {'chip'}, use_global_device_ids=true, to_apply=%region_4.5 | all-reduce | flops 128 | bytes 1024 | tf_op jit(solution)/shard_map/psum | solution.py:56
  559.6 9.7 %all_gather.7 = bf16[128,1024]{1,0:T(8,128)(2,1)S(1)} all-gather(bf16[128,256]{1,0:T(8,128)(2,1)S(1)} %multiply_convert_fusion), channel_id=1, replica_groups=mesh['hst'=64,'chip'=4] {'chip'}, dimensions={1}, use_global_device_ids=true | all-gather | bytes 327680 | tf_op jit(solution)/shard_map/all_gather | solution.py:59
  569.3 14.6 %collective-permute-done = bf16[128,1024]{1,0:T(8,128)(2,1)S(1)} collective-permute-done((bf16[128,1024]{1,0:T(8,128)(2,1)S(1)}, bf16[128,1024]{1,0:T(8,128)(2,1)S(1)}, u32[]{:S(2)}, u32[]{:S(2)}) %collective-permute-start) | collective-permute-done | bytes 262176 | tf_op jit(solution)/shard_map/ppermute | solution.py:25
  583.8 13.7 %collective-permute-done.1 = bf16[128,1024]{1,0:T(8,128)(2,1)S(1)} collective-permute-done((bf16[128,1024]{1,0:T(8,128)(2,1)S(1)}, bf16[128,1024]{1,0:T(8,128)(2,1)S(1)}, u32[]{:S(2)}, u32[]{:S(2)}) %collective-permute-start.1) | collective-permute-done | bytes 262176 | tf_op jit(solution)/shard_map/ppermute | solution.py:25
  597.8 12.6 %collective-permute-done.2 = bf16[128,1024]{1,0:T(8,128)(2,1)S(1)} collective-permute-done((bf16[128,1024]{1,0:T(8,128)(2,1)S(1)}, bf16[128,1024]{1,0:T(8,128)(2,1)S(1)}, u32[]{:S(2)}, u32[]{:S(2)}) %collective-permute-start.2) | collective-permute-done | bytes 262176 | tf_op jit(solution)/shard_map/ppermute | solution.py:25
  611.0 11.8 %collective-permute-done.3 = bf16[128,1024]{1,0:T(8,128)(2,1)S(1)} collective-permute-done((bf16[128,1024]{1,0:T(8,128)(2,1)S(1)}, bf16[128,1024]{1,0:T(8,128)(2,1)S(1)}, u32[]{:S(2)}, u32[]{:S(2)}) %collective-permute-start.3) | collective-permute-done | bytes 262176 | tf_op jit(solution)/shard_map/ppermute | solution.py:25
  624.0 11.2 %collective-permute-done.4 = bf16[128,1024]{1,0:T(8,128)(2,1)S(1)} collective-permute-done((bf16[128,1024]{1,0:T(8,128)(2,1)S(1)}, bf16[128,1024]{1,0:T(8,128)(2,1)S(1)}, u32[]{:S(2)}, u32[]{:S(2)}) %collective-permute-start.4) | collective-permute-done | bytes 262176 | tf_op jit(solution)/shard_map/ppermute | solution.py:25
  636.4 11.2 %collective-permute-done.5 = bf16[128,1024]{1,0:T(8,128)(2,1)S(1)} collective-permute-done((bf16[128,1024]{1,0:T(8,128)(2,1)S(1)}, bf16[128,1024]{1,0:T(8,128)(2,1)S(1)}, u32[]{:S(2)}, u32[]{:S(2)}) %collective-permute-start.5) | collective-permute-done | bytes 262176 | tf_op jit(solution)/shard_map/ppermute | solution.py:25
  648.7 11.2 %collective-permute-done.6 = bf16[128,1024]{1,0:T(8,128)(2,1)S(1)} collective-permute-done((bf16[128,1024]{1,0:T(8,128)(2,1)S(1)}, bf16[128,1024]{1,0:T(8,128)(2,1)S(1)}, u32[]{:S(2)}, u32[]{:S(2)}) %collective-permute-start.6) | collective-permute-done | bytes 262176 | tf_op jit(solution)/shard_map/ppermute | solution.py:25
  (47 shorter events, 16.4 us)
Async XLA Ops:
  10.9 6.9 %copy-start.2 = (s32[512]{0:T(512)S(1)}, s32[512]{0:T(512)}, u32[]{:S(2)}) copy-start(s32[512]{0:T(512)} %param.5) | copy-start | bytes 6148
  10.9 104.5 %all-to-all-start = ((bf16[4,512,1024]{2,1,0:T(8,128)(2,1)}), bf16[4,512,1024]{2,1,0:T(8,128)(2,1)}, u32[]{:S(2)}, u32[]{:S(2)}) async-start(bf16[4,512,1024]{2,1,0:T(8,128)(2,1)} %stack.2), calls=%async_computation | async-start | bytes 8388608 | tf_op jit(solution)/shard_map/all_to_all | solution.py:14
  17.8 530.2 %reduce-scatter.2.cloned.1.call-start = ((), (), s32[]{:S(2)}) async-start(), calls=%async_computation.2 | async-start | bytes 8519680 | tf_op jit(solution)/shard_map/reduce_scatter | solution.py:50
  145.1 452.4 %copy-start = (bf16[512,1024]{1,0:T(8,128)(2,1)S(1)}, bf16[512,1024]{1,0:T(8,128)(2,1)}, u32[]{:S(2)}) copy-start(bf16[512,1024]{1,0:T(8,128)(2,1)} %param.4) | copy-start | bytes 3145732
  559.6 63.8 %copy-start.1 = (bf16[128,256]{1,0:T(8,128)(2,1)}, bf16[128,256]{1,0:T(8,128)(2,1)S(1)}, u32[]{:S(2)}) copy-start(bf16[128,256]{1,0:T(8,128)(2,1)S(1)} %multiply_convert_fusion) | copy-start | bytes 196612
  569.3 14.6 %collective-permute-start = (bf16[128,1024]{1,0:T(8,128)(2,1)S(1)}, bf16[128,1024]{1,0:T(8,128)(2,1)S(1)}, u32[]{:S(2)}, u32[]{:S(2)}) collective-permute-start(bf16[128,1024]{1,0:T(8,128)(2,1)S(1)} %all_gather.7), channel_id=1, source_target_pairs={{252,0},{0,4},{4,8},{8,12},{12,16},{16,20},{20,24},{24,28},{28,32}... | collective-permute-start | bytes 786440 | tf_op jit(solution)/shard_map/ppermute | solution.py:25
  583.8 13.7 %collective-permute-start.1 = (bf16[128,1024]{1,0:T(8,128)(2,1)S(1)}, bf16[128,1024]{1,0:T(8,128)(2,1)S(1)}, u32[]{:S(2)}, u32[]{:S(2)}) collective-permute-start(bf16[128,1024]{1,0:T(8,128)(2,1)S(1)} %collective-permute-done), channel_id=1, source_target_pairs={{252,0},{0,4},{4,8},{8,12},{12,16},{16,20},{20,24},{24,28},{28,32}... | collective-permute-start | bytes 786440 | tf_op jit(solution)/shard_map/ppermute | solution.py:25
  597.6 12.9 %collective-permute-start.2 = (bf16[128,1024]{1,0:T(8,128)(2,1)S(1)}, bf16[128,1024]{1,0:T(8,128)(2,1)S(1)}, u32[]{:S(2)}, u32[]{:S(2)}) collective-permute-start(bf16[128,1024]{1,0:T(8,128)(2,1)S(1)} %collective-permute-done.1), channel_id=1, source_target_pairs={{252,0},{0,4},{4,8},{8,12},{12,16},{16,20},{20,24},{24,28},{28,32}... | collective-permute-start | bytes 786440 | tf_op jit(solution)/shard_map/ppermute | solution.py:25
  610.4 12.4 %collective-permute-start.3 = (bf16[128,1024]{1,0:T(8,128)(2,1)S(1)}, bf16[128,1024]{1,0:T(8,128)(2,1)S(1)}, u32[]{:S(2)}, u32[]{:S(2)}) collective-permute-start(bf16[128,1024]{1,0:T(8,128)(2,1)S(1)} %collective-permute-done.2), channel_id=1, source_target_pairs={{252,0},{0,4},{4,8},{8,12},{12,16},{16,20},{20,24},{24,28},{28,32}... | collective-permute-start | bytes 786440 | tf_op jit(solution)/shard_map/ppermute | solution.py:25
  622.8 12.4 %collective-permute-start.4 = (bf16[128,1024]{1,0:T(8,128)(2,1)S(1)}, bf16[128,1024]{1,0:T(8,128)(2,1)S(1)}, u32[]{:S(2)}, u32[]{:S(2)}) collective-permute-start(bf16[128,1024]{1,0:T(8,128)(2,1)S(1)} %collective-permute-done.3), channel_id=1, source_target_pairs={{252,0},{0,4},{4,8},{8,12},{12,16},{16,20},{20,24},{24,28},{28,32}... | collective-permute-start | bytes 786440 | tf_op jit(solution)/shard_map/ppermute | solution.py:25
  635.2 12.4 %collective-permute-start.5 = (bf16[128,1024]{1,0:T(8,128)(2,1)S(1)}, bf16[128,1024]{1,0:T(8,128)(2,1)S(1)}, u32[]{:S(2)}, u32[]{:S(2)}) collective-permute-start(bf16[128,1024]{1,0:T(8,128)(2,1)S(1)} %collective-permute-done.4), channel_id=1, source_target_pairs={{252,0},{0,4},{4,8},{8,12},{12,16},{16,20},{20,24},{24,28},{28,32}... | collective-permute-start | bytes 786440 | tf_op jit(solution)/shard_map/ppermute | solution.py:25
  647.6 12.4 %collective-permute-start.6 = (bf16[128,1024]{1,0:T(8,128)(2,1)S(1)}, bf16[128,1024]{1,0:T(8,128)(2,1)S(1)}, u32[]{:S(2)}, u32[]{:S(2)}) collective-permute-start(bf16[128,1024]{1,0:T(8,128)(2,1)S(1)} %collective-permute-done.5), channel_id=1, source_target_pairs={{252,0},{0,4},{4,8},{8,12},{12,16},{16,20},{20,24},{24,28},{28,32}... | collective-permute-start | bytes 786440 | tf_op jit(solution)/shard_map/ppermute | solution.py:25
Sparse Core Ops, SparseCore 0:
  145.3 402.6 reduce-scatter.1
